TPU v7x, 512 devices: a whole 4x8x8 slice. The times are simulated.
512 devices in a mesh: blk: 16 (over x_lo, y), exp: 32 (over z, x_hi, core).
Axes of the slice: x: 4 (x_hi: 2, x_lo: 2; x = x_hi * 2 + x_lo), y: 8, z: 8, core: 2. Of those that a mesh axis runs over, the one named last changes fastest.
Arguments:
- residual: bfloat16 [32, 2048, 1024], P('exp', 'blk'), may hold values from -6 to 6
- queries: bfloat16 [32, 2048, 1024], P('exp', 'blk'), may hold values from -6 to 6
- suffix_kv: bfloat16 [32, 2048, 1024], P('exp', 'blk'), may hold values from -6 to 6
- prompt_kv: bfloat16 [32, 1024, 1024], P('exp', 'blk'), may hold values from -6 to 6
- prompt_lengths: int32 [32], P('exp'), may hold values from 1 to 1024, as said below
- block_keep: int32 [32, 32], P('exp', 'blk'), may hold values 0 or 1
- suffix_lengths: int32 [32, 16, 4], P('exp', 'blk'), may hold values from 1 to 64, 128 in all within a row
- out_weight: bfloat16 [1024, 1024], P('exp'), may hold values from -0.75 to 0.75
- routes: int32 [32, 2048, 8], P('exp', 'blk'), may hold values from 0 to 31, all different within a row; in each aligned block of 128 rows (0 to 127, 128 to 255, ..., all dimensions but the last counted through in order) at most 40 rows name the same one
- route_weight: float32 [32, 2048, 8], P('exp', 'blk'), may hold values from 0.02 to 0.25
- gate_up_weight: bfloat16 [32, 1024, 1024], P('exp'), may hold values from -0.1875 to 0.1875
- down_weight: bfloat16 [32, 512, 1024], P('exp'), may hold values from -0.25 to 0.25
- page_owner: int32 [32, 128, 1], P('exp', 'blk'), may hold values from 0 to 15; in each aligned block of 8 rows (0 to 7, 8 to 15, ..., all dimensions but the last counted through in order) at most 2 rows name the same one
Outputs:
- attended: bfloat16 [32, 2048, 1024], P('exp', 'blk')
- layer_out: bfloat16 [32, 2048, 1024], P('exp', 'blk')
- cache_pages: bfloat16 [32, 4096, 1024], P('exp', 'blk')
Inputs may be any that keep to these rules, and one draw needn't show every extreme that they name: `prompt_lengths`: some group's prompt length equals 1024. `suffix_lengths`: each device's 4 request lengths sum to 128. `routes`: each token names 8 different experts; among the tokens of one device at most 40 name any one expert, and that bound is reached. `page_owner`: among the 8 pages of one device at most 2 go to any one owner, and that bound is reached.
All inputs are finite; a program needn't handle non-finite values. No bound on the sum of `block_keep` on one device may be relied on, other than what follows from the above.
Results may differ from a plain program's by a relative error of at most 0.013.
Values may be sent and summed in bfloat16 or wider, within the bound.
No kernel may reach another device: no remote copies, remote signals or barrier semaphores. Data moves between devices by JAX's collectives and lax.ppermute only.
A program may use at most 64 MiB of HBM per device.

v0:
```python
import jax
import jax.numpy as jnp
from jax import lax
from jax.sharding import PartitionSpec as P

D = 1024
H = 16
KVH = 8
HD = 64
FF = 512
TOPK = 8
EXP_DEV = 1
KB = 32
PAGE = 8
SCALE = 0.125
NEGATIVE = -1e30
EPSILON = 1e-06


def segment_of(lengths, count):
    ends = jnp.cumsum(lengths)
    position = jnp.arange(count, dtype=jnp.int32)
    return jnp.sum((position[:, None] >= ends[None, :]).astype(jnp.int32), axis=1)


def rank_within(labels, count):
    onehot = (labels[:, None] == jnp.arange(count, dtype=jnp.int32)[None, :]).astype(jnp.int32)
    before = jnp.cumsum(onehot, axis=0) - onehot
    return jnp.sum(before * onehot, axis=1)


def gather_rows(piece, axis):
    count = lax.axis_size(axis)
    tiles = jnp.broadcast_to(piece[None], (count,) + piece.shape)
    whole = lax.all_to_all(tiles, axis, split_axis=0, concat_axis=0, tiled=True)
    return whole.reshape((count * piece.shape[0],) + piece.shape[1:])


def absorb(carry_state, query_heads, key_heads, value_heads, visible):
    running_max, denom, numerator = carry_state
    scores = (
        jnp.einsum("tkgd,skd->tkgs", query_heads, key_heads, preferred_element_type=jnp.float32)
        * SCALE
    )
    new_max = jnp.maximum(running_max, jnp.max(jnp.where(visible, scores, NEGATIVE), axis=-1))
    factor = jnp.exp(running_max - new_max)
    weight = jnp.where(visible, jnp.exp(scores - new_max[..., None]), 0.0)
    denom = denom * factor + jnp.sum(weight, axis=-1)
    added = jnp.einsum(
        "tkgs,skd->tkgd",
        weight.astype(jnp.bfloat16),
        value_heads,
        preferred_element_type=jnp.float32,
    )
    numerator = numerator * factor[..., None] + added
    return (new_max, denom, numerator)


def local(
    residual,
    queries,
    suffix_kv,
    prompt_kv,
    prompt_lengths,
    block_keep,
    suffix_lengths,
    out_weight,
    routes,
    route_weight,
    gate_up_weight,
    down_weight,
    page_owner,
):
    tok_rows = queries.shape[1]
    kv_width = suffix_kv.shape[2] // 2
    group_size = H // KVH
    query_heads = queries[0].reshape(tok_rows, KVH, group_size, HD)
    own_keys = suffix_kv[0, :, :kv_width].reshape(tok_rows, KVH, HD)
    own_values = suffix_kv[0, :, kv_width:].reshape(tok_rows, KVH, HD)
    segment = segment_of(suffix_lengths[0, 0], tok_rows)
    position = jnp.arange(tok_rows, dtype=jnp.int32)
    own_seen = ((segment[:, None] == segment[None, :]) & (position[None, :] <= position[:, None]))[
        :, None, None, :
    ]
    start_state = (
        jnp.full((tok_rows, KVH, group_size), NEGATIVE, jnp.float32),
        jnp.zeros((tok_rows, KVH, group_size), jnp.float32),
        jnp.zeros((tok_rows, KVH, group_size, HD), jnp.float32),
    )
    carry_state = absorb(start_state, query_heads, own_keys, own_values, own_seen)
    block_rows = prompt_kv.shape[1]
    keep_rows = jnp.repeat(block_keep[0], KB)
    position_abs = lax.axis_index("blk") * block_rows + jnp.arange(block_rows, dtype=jnp.int32)
    live_keys = ((keep_rows > 0) & (position_abs < prompt_lengths[0])).astype(jnp.int32)[None, :]
    piece_kv = lax.all_gather(prompt_kv, "blk", axis=1, tiled=True)
    blk_count = lax.axis_size("blk")
    page_count = block_rows // PAGE
    packed = jnp.concatenate([live_keys[0], page_owner[0, :, 0]])
    packed_all = lax.all_gather(packed, "blk", axis=0, tiled=True).reshape(blk_count, -1)
    piece_live = packed_all[:, :block_rows].reshape(1, -1)
    owners_all = packed_all[:, block_rows:]
    count = piece_kv.shape[1]
    key_heads = piece_kv[0, :, :kv_width].reshape(count, KVH, HD)
    value_heads = piece_kv[0, :, kv_width:].reshape(count, KVH, HD)
    visible = (piece_live[0] > 0)[None, None, None, :]
    running_max, denom, numerator = absorb(
        carry_state, query_heads, key_heads, value_heads, visible
    )
    attended = (numerator / denom[..., None]).reshape(tok_rows, H * HD).astype(jnp.bfloat16)
    projected = jnp.dot(
        attended, gather_rows(out_weight, "exp"), preferred_element_type=jnp.float32
    )
    stream = (residual[0].astype(jnp.float32) + projected).astype(jnp.bfloat16)
    stream_f32 = stream.astype(jnp.float32)
    normed = (
        stream_f32 * lax.rsqrt(jnp.mean(stream_f32 * stream_f32, axis=-1, keepdims=True) + EPSILON)
    ).astype(jnp.bfloat16)
    exp_count = lax.axis_size("exp")
    experts = EXP_DEV * exp_count
    capacity = min(tok_rows, 5 * tok_rows * TOPK // (4 * experts))
    flat_routes = routes[0].reshape(-1)
    slot_index = flat_routes * capacity + rank_within(flat_routes, experts)
    slot_iota = jnp.arange(experts * capacity, dtype=jnp.int32)
    token_slots = slot_index.reshape(tok_rows, TOPK)
    hits = token_slots[None, :, :] == slot_iota[:, None, None]
    placer = jnp.any(hits, axis=-1).astype(jnp.bfloat16)
    dispatch = jnp.dot(placer, normed, preferred_element_type=jnp.float32).astype(jnp.bfloat16)
    dispatch = dispatch.reshape(experts, capacity, D)
    arrived = lax.all_to_all(dispatch, "exp", split_axis=0, concat_axis=0, tiled=True)
    count = arrived.shape[1]
    grouped = arrived.reshape(exp_count, EXP_DEV, count, D)
    picked_rows = grouped[:, 0].reshape(exp_count * count, D)
    gate_up = jnp.dot(picked_rows, gate_up_weight[0], preferred_element_type=jnp.float32)
    hidden = (jax.nn.silu(gate_up[:, :FF]) * gate_up[:, FF:]).astype(jnp.bfloat16)
    result = jnp.dot(hidden, down_weight[0], preferred_element_type=jnp.float32).astype(
        jnp.bfloat16
    )
    results = [result.reshape(exp_count, count, D)]
    outgoing = jnp.stack(results, axis=1).reshape(exp_count * EXP_DEV, count, D)
    returned = lax.all_to_all(outgoing, "exp", split_axis=0, concat_axis=0, tiled=True)
    slot_weight = jnp.sum(
        jnp.where(
            token_slots[:, :, None] == slot_iota[None, None, :], route_weight[0][:, :, None], 0.0
        ),
        axis=1,
    )
    combined = jnp.dot(
        slot_weight,
        returned.reshape(experts * capacity, D).astype(jnp.float32),
        precision=lax.Precision.HIGH,
        preferred_element_type=jnp.float32,
    )
    layer_out = (stream_f32 + combined).astype(jnp.bfloat16)
    page_capacity = max(2, 2 * page_count // blk_count)
    me = lax.axis_index("blk")
    page_rank = jax.vmap(lambda labels: rank_within(labels, blk_count))(owners_all)
    block_of = jnp.arange(blk_count, dtype=jnp.int32)[:, None]
    page_slot = jnp.where(owners_all == me, block_of * page_capacity + page_rank, -1).reshape(-1)
    out_rows = blk_count * page_capacity * PAGE
    row_slot = jnp.arange(out_rows, dtype=jnp.int32) // PAGE
    prompt_rows = piece_kv.shape[1]
    src_page = jnp.arange(prompt_rows, dtype=jnp.int32) // PAGE
    same_row = jnp.arange(out_rows)[:, None] % PAGE == jnp.arange(prompt_rows)[None, :] % PAGE
    chooser = (page_slot[src_page][None, :] == row_slot[:, None]) & same_row
    cache_pages = jnp.dot(
        chooser.astype(jnp.bfloat16), piece_kv[0], preferred_element_type=jnp.float32
    ).astype(jnp.bfloat16)[None]
    return (attended[None], layer_out[None], cache_pages)


def solution(mesh):
    return jax.shard_map(
        local,
        mesh=mesh,
        in_specs=(
            P("exp", "blk", None),
            P("exp", "blk", None),
            P("exp", "blk", None),
            P("exp", "blk", None),
            P("exp"),
            P("exp", "blk"),
            P("exp", "blk", None),
            P("exp", None),
            P("exp", "blk", None),
            P("exp", "blk", None),
            P("exp", None, None),
            P("exp", None, None),
            P("exp", "blk", None),
        ),
        out_specs=(P("exp", "blk", None), P("exp", "blk", None), P("exp", "blk", None)),
        check_vma=False,
    )
```

profile of v0, /device:TPU:8, one launch (start us, length us, event | category | flops | bytes accessed | tf_op | source)
XLA Modules:
  0.0 263.8 jit_solution(6552238439701241968)
XLA Ops:
  7.2 0.7 all-gather.2.cloned.1.call-update
  7.9 2.4 broadcast_in_dim.111
  10.3 13.4 %all-to-all-start = ((bf16[32,32,1024]{2,1,0:T(8,128)(2,1)}), bf16[32,32,1024]{2,1,0:T(8,128)(2,1)}, u32[]{:S(2)}, u32[]{:S(2)}) async-start(bf16[32,32,1024]{2,1,0:T(8,128)(2,1)} %broadcast_in_dim.111), calls=%async_computation | async-start | bytes 4194304 | tf_op jit(solution)/shard_map/all_to_all | solution.py:35
  24.9 1.3 dynamic-slice
  27.1 15.8 %all-reduce = s32[1152]{0:T(1024)S(1)} all-reduce(s32[1152]{0:T(1024)S(1)} %add_dynamic-update-slice_fusion), channel_id=1, replica_groups=mesh['blk'=16,'exp'=32] {'blk'}, use_global_device_ids=true, to_apply=%add | all-reduce | flops 1152 | bytes 9216
  43.6 0.8 copy.44
  44.4 9.0 %reduce-window.19 = s32[32,8,128]{2,1,0:T(8,128)S(1)} reduce-window(s32[32,8,128]{2,1,0:T(8,128)S(1)} %fusion.52, s32[]{:T(128)} %constant.83.clone.1), window={size=1x1x128 pad=0_0x0_0x127_0}, to_apply=%region_6.7 | reduce-window | flops 4161536 | bytes 262148 | tf_op jit(solution)/shard_map/reduce-window.1
  54.2 5.3 %fusion.5 = pred[1280,128]{1,0:T(8,128)(4,1)} fusion(s32[128,8]{0,1:T(8,128)S(1)} %copy.55), kind=kLoop, calls=%fused_computation.11 | loop fusion | flops 2457600 | bytes 167936 | tf_op jit(solution)/shard_map/reduce_or | solution.py:126
  59.6 1.3 select_reduce_fusion.1
  60.9 29.1 %all-gather.2.cloned.1.call-done = bf16[1,1024,1024]{2,1,0:T(8,128)(2,1)} async-done(((bf16[1,64,1024]{2,1,0:T(8,128)(2,1)}), bf16[1,1024,1024]{2,1,0:T(8,128)(2,1)}) %all-gather.2.cloned.1.call-update) | async-done | bytes 2097168 | tf_op jit(solution)/shard_map/all_gather | solution.py:95
  90.0 2.7 %fusion.65 = (bf16[1,1024,512]{2,1,0:T(8,128)(2,1)}, bf16[1,1024,512]{2,1,0:T(8,128)(2,1)S(1)}) fusion(bf16[1,1024,1024]{2,1,0:T(8,128)(2,1)} %all-gather.2.cloned.1.call-done), kind=kLoop, calls=%fused_computation.108 | loop fusion | bytes 4194304 | tf_op jit(solution)/shard_map/slice | solution.py:103
  92.7 1.3 copy.47
  94.1 1.5 copy.46
  95.6 2.2 fusion
  97.8 0.2 fusion.38
  98.0 2.2 fusion.3
  100.3 1.5 fusion.22
  101.9 0.3 fusion.30
  102.2 0.6 copy-done.7
  102.8 2.1 multiply_reduce_fusion
  105.0 0.9 convolution_convert_fusion.1
  105.9 73.8 %all_to_all.15 = bf16[32,40,1024]{2,1,0:T(8,128)(2,1)S(1)} all-to-all(bf16[32,40,1024]{2,1,0:T(8,128)(2,1)S(1)} %bitcast.124), channel_id=1, replica_groups=mesh['blk'=16,'exp'=32] {'exp'}, dimensions={0} | all-to-all | bytes 5242880 | tf_op jit(solution)/shard_map/all_to_all | solution.py:129
  179.7 2.9 %fusion.12 = f32[1280,1024]{1,0:T(8,128)S(1)} fusion(bf16[1280,1024]{1,0:T(8,128)(2,1)S(1)} %bitcast.127, bf16[1,1024,1024]{2,1,0:T(8,128)(2,1)S(1)} %copy-done), kind=kOutput, calls=%fused_computation.20 | convolution fusion | flops 2684354560 | bytes 9961472 | tf_op jit(solution)/shard_map/dot_general | solution.py:133
  182.6 3.1 %convolution_convert_fusion = bf16[1280,1024]{1,0:T(8,128)(2,1)} fusion(f32[1280,1024]{1,0:T(8,128)S(1)} %fusion.12, bf16[1,512,1024]{2,1,0:T(8,128)(2,1)S(1)} %copy-done.12), kind=kOutput, calls=%fused_computation.14 | convolution fusion | flops 1347420160 | bytes 8912896 | tf_op jit(solution)/shard_map/dot_general | solution.py:135
  185.7 4.9 %all-to-all-start.2 = ((bf16[32,40,1024]{2,1,0:T(8,128)(2,1)}), bf16[32,40,1024]{2,1,0:T(8,128)(2,1)}, u32[]{:S(2)}, u32[]{:S(2)}) async-start(bf16[32,40,1024]{2,1,0:T(8,128)(2,1)} %bitcast.126), calls=%async_computation.2 | async-start | bytes 5242880 | tf_op jit(solution)/shard_map/all_to_all | solution.py:140
  191.1 0.4 select_reduce_fusion.2
  191.7 6.6 %gather_fusion = s32[1024]{0:T(1024)S(1)} fusion(s32[128]{0:T(128)S(1)} %reshape.278, s32[1024]{0:T(1024)S(1)} %broadcast_clamp_fusion), kind=kCustom, calls=%fused_computation | custom fusion | bytes 12288 | tf_op jit(solution)/shard_map/gather | solution.py:164
  198.3 1.6 select_reduce_fusion
  200.0 1.8 copy.56
  201.8 3.1 %fusion.19 = bf16[1,256,1024]{2,1,0:T(8,128)(2,1)} fusion(bf16[1,1024,1024]{2,1,0:T(8,128)(2,1)} %all-gather.2.cloned.1.call-done, s32[1024]{0:T(1024)S(1)} %add_select_fusion.1, s32[1024]{0:T(1024)S(1)} %gather_fusion, s32[256]{0:T(256)S(1)} %get-tuple-element.27, s32[256]{0:T(256)S(1)} %get-tuple-element.28), kind=kOutput, calls=%fused_computation.26 | convolution fusion | flops 537919488 | bytes 2631680 | tf_op jit(solution)/shard_map/dot_general | solution.py:165
  204.9 48.7 %all-to-all-done.2 = bf16[32,40,1024]{2,1,0:T(8,128)(2,1)} async-done(((bf16[32,40,1024]{2,1,0:T(8,128)(2,1)}), bf16[32,40,1024]{2,1,0:T(8,128)(2,1)}, u32[]{:S(2)}, u32[]{:S(2)}) %all-to-all-start.2) | async-done | bytes 2621472 | tf_op jit(solution)/shard_map/all_to_all | solution.py:140
  253.6 3.3 %fusion.33 = bf16[1,128,1024]{2,1,0:T(8,128)(2,1)} fusion(f32[128,1024]{1,0:T(8,128)S(1)} %get-tuple-element.26, f32[128,1280]{1,0:T(8,128)S(1)} %select_reduce_fusion, bf16[1280,1024]{1,0:T(8,128)(2,1)} %bitcast.37), kind=kOutput, calls=%fused_computation.38 | convolution fusion | flops 1006895104 | bytes 4063232 | tf_op jit(solution)/shard_map/dot_general | solution.py:147
  (76 shorter events, 2.9 us)
Async XLA Ops:
  7.2 172.5 %copy-start = (bf16[1,1024,1024]{2,1,0:T(8,128)(2,1)S(1)}, bf16[1,1024,1024]{2,1,0:T(8,128)(2,1)}, u32[]{:S(2)}) copy-start(bf16[1,1024,1024]{2,1,0:T(8,128)(2,1)} %param.23) | copy-start | bytes 6291460
  7.2 82.8 %all-gather.2.cloned.1.call-start = ((), (), s32[]{:S(2)}) async-start(), calls=%async_computation.3 | async-start | bytes 2228224 | tf_op jit(solution)/shard_map/all_gather | solution.py:95
  10.3 13.5 %copy-start.9 = (s32[1,128,8]{1,2,0:T(8,128)S(1)}, s32[1,128,8]{1,2,0:T(8,128)}, u32[]{:S(2)}) copy-start(s32[1,128,8]{1,2,0:T(8,128)} %param.21) | copy-start | bytes 12292
  10.3 13.8 %copy-start.13 = (s32[1,2]{1,0:T(1,128)S(1)}, s32[1,2]{1,0:T(1,128)}, u32[]{:S(2)}) copy-start(s32[1,2]{1,0:T(1,128)} %param.18) | copy-start | bytes 28
  10.3 16.6 %copy-start.11 = (s32[1,8,1]{1,2,0:T(1,128)S(1)}, s32[1,8,1]{1,2,0:T(1,128)}, u32[]{:S(2)}) copy-start(s32[1,8,1]{1,2,0:T(1,128)} %param.25) | copy-start | bytes 100
  10.3 32.8 %copy-start.5 = (bf16[1,128,1024]{2,1,0:T(8,128)(2,1)S(1)}, bf16[1,128,1024]{2,1,0:T(8,128)(2,1)}, u32[]{:S(2)}) copy-start(bf16[1,128,1024]{2,1,0:T(8,128)(2,1)} %param.14) | copy-start | bytes 786436
  10.3 33.0 %copy-start.14 = (s32[1,1,4]{2,1,0:T(1,128)S(1)}, s32[1,1,4]{2,1,0:T(1,128)}, u32[]{:S(2)}) copy-start(s32[1,1,4]{2,1,0:T(1,128)} %param.19) | copy-start | bytes 52
  10.3 33.1 %copy-start.6 = (bf16[1,128,1024]{2,1,0:T(8,128)(2,1)S(1)}, bf16[1,128,1024]{2,1,0:T(8,128)(2,1)}, u32[]{:S(2)}) copy-start(bf16[1,128,1024]{2,1,0:T(8,128)(2,1)} %param.15) | copy-start | bytes 786436
  10.3 91.9 %all-to-all-start = ((bf16[32,32,1024]{2,1,0:T(8,128)(2,1)}), bf16[32,32,1024]{2,1,0:T(8,128)(2,1)}, u32[]{:S(2)}, u32[]{:S(2)}) async-start(bf16[32,32,1024]{2,1,0:T(8,128)(2,1)} %broadcast_in_dim.111), calls=%async_computation | async-start | bytes 4194304 | tf_op jit(solution)/shard_map/all_to_all | solution.py:35
  95.6 2.3 copy-start.1
  98.0 2.3 copy-start.2
  100.3 1.6 copy-start.8
  101.9 1.0 copy-start.7
  101.9 3.1 %copy-start.4 = (pred[1280,128]{1,0:T(8,128)(4,1)S(1)}, pred[1280,128]{1,0:T(8,128)(4,1)}, u32[]{:S(2)}) copy-start(pred[1280,128]{1,0:T(8,128)(4,1)} %fusion.5) | copy-start | bytes 491524
  102.2 3.7 %copy-start.3 = (bf16[128,8,2,64]{0,3,2,1:T(8,128)(2,1)}, bf16[128,8,2,64]{0,3,2,1:T(8,128)(2,1)S(1)}, u32[]{:S(2)}) copy-start(bf16[128,8,2,64]{0,3,2,1:T(8,128)(2,1)S(1)} %fusion.30) | copy-start | bytes 786436
  179.7 2.9 %copy-start.12 = (bf16[1,512,1024]{2,1,0:T(8,128)(2,1)S(1)}, bf16[1,512,1024]{2,1,0:T(8,128)(2,1)}, u32[]{:S(2)}) copy-start(bf16[1,512,1024]{2,1,0:T(8,128)(2,1)} %param.24) | copy-start | bytes 3145732
  185.7 5.1 %copy-start.10 = (f32[1,128,8]{1,2,0:T(8,128)S(1)}, f32[1,128,8]{1,2,0:T(8,128)}, u32[]{:S(2)}) copy-start(f32[1,128,8]{1,2,0:T(8,128)} %param.22) | copy-start | bytes 12292
  185.7 67.9 %all-to-all-start.2 = ((bf16[32,40,1024]{2,1,0:T(8,128)(2,1)}), bf16[32,40,1024]{2,1,0:T(8,128)(2,1)}, u32[]{:S(2)}, u32[]{:S(2)}) async-start(bf16[32,40,1024]{2,1,0:T(8,128)(2,1)} %bitcast.126), calls=%async_computation.2 | async-start | bytes 5242880 | tf_op jit(solution)/shard_map/all_to_all | solution.py:140
Sparse Core Ops, SparseCore 0:
  10.1 79.8 all-gather.1
where the time goes:
time: 264 us
  blocking collectives  89.6 us (34%)
  waiting for transfers between devices  78.5 us (30%)
  matrix products  20.9 us (8%)
  local copies, waits for them, and re-layouts  20.7 us (8%)
  other arithmetic  19.9 us (8%)
  starting transfers between devices  18.4 us (7%)
  between operations  15.8 us (6%)
    all_to_all x1, blocking collectives, local(): lax.all_to_all(dispatch, 'exp', split_axis=0, concat_axis=0, tiled=True)  73.8 us
    all_to_all x1, waiting for transfers between devices, local(): lax.all_to_all(outgoing, 'exp', split_axis=0, concat_axis=0, tiled=True)  48.7 us
    all_gather x1, waiting for transfers between devices, local(): piece_kv = lax.all_gather(prompt_kv, 'blk', axis=1, tiled=True)  29.1 us
    unnamed x1, blocking collectives  15.8 us
    all_to_all x1, starting transfers between devices, gather_rows(): whole = lax.all_to_all(tiles, axis, split_axis=0, concat_axis=0, tiled=True)  13.4 us
    another operation x4, other arithmetic  9.33 us
    gather x1, local copies, waits for them, and re-layouts, local(): chooser = (page_slot[src_page][None, :] == row_slot[:, None]) & same_row  6.57 us
    reduce_or x1, other arithmetic, local(): placer = jnp.any(hits, axis=-1).astype(jnp.bfloat16)  5.32 us
  transfers between devices with their start and end apart: 3, of which 2 were waited for; matrix products, arithmetic and copies ran while one was open for 18% of the time, Pallas kernels for 0%

commit v1 on v0

--- a/solution.py
+++ b/solution.py
@@ -15,6 +15,13 @@
 SCALE = 0.125
 NEGATIVE = -1e30
 EPSILON = 1e-06
+
+
+def gather_over(x, axis, d):
+    size = lax.axis_size(axis)
+    blocks = jnp.stack([x for _ in range(size)])
+    blocks = lax.all_to_all(blocks, axis, split_axis=0, concat_axis=0)
+    return jnp.concatenate(blocks, axis=d)
 
 
 def segment_of(lengths, count):
@@ -92,7 +99,7 @@
     keep_rows = jnp.repeat(block_keep[0], KB)
     position_abs = lax.axis_index("blk") * block_rows + jnp.arange(block_rows, dtype=jnp.int32)
     live_keys = ((keep_rows > 0) & (position_abs < prompt_lengths[0])).astype(jnp.int32)[None, :]
-    piece_kv = lax.all_gather(prompt_kv, "blk", axis=1, tiled=True)
+    piece_kv = gather_over(prompt_kv, "blk", 1)
     blk_count = lax.axis_size("blk")
     page_count = block_rows // PAGE
     packed = jnp.concatenate([live_keys[0], page_owner[0, :, 0]])

time: 264 us -> 297 us (1.12)
  the two profiles are of different devices: /device:TPU:8 before, /device:TPU:16 now
where the time goes in v1:
time: 297 us; the launch traced here: 296 us
  blocking collectives  123 us (41%)
  waiting for transfers between devices  79.7 us (27%)
  starting transfers between devices  28.6 us (10%)
  local copies, waits for them, and re-layouts  21.9 us (7%)
  matrix products  20.9 us (7%)
  other arithmetic  19.9 us (7%)
    all_to_all x1, blocking collectives, local(): lax.all_to_all(dispatch, 'exp', split_axis=0, concat_axis=0, tiled=True)  69.1 us
    unnamed x1, blocking collectives  53.6 us
    all_to_all x1, waiting for transfers between devices, local(): lax.all_to_all(outgoing, 'exp', split_axis=0, concat_axis=0, tiled=True)  48.7 us
    all_to_all x1, waiting for transfers between devices, gather_rows(): whole = lax.all_to_all(tiles, axis, split_axis=0, concat_axis=0, tiled=True)  31 us
    all_to_all x1, starting transfers between devices, gather_rows(): whole = lax.all_to_all(tiles, axis, split_axis=0, concat_axis=0, tiled=True)  13.6 us
    all_to_all x1, starting transfers between devices, gather_over(): blocks = lax.all_to_all(blocks, axis, split_axis=0, concat_axis=0)  10 us
    another operation x4, other arithmetic  9.33 us
    gather x1, local copies, waits for them, and re-layouts, local(): chooser = (page_slot[src_page][None, :] == row_slot[:, None]) & same_row  6.57 us
  transfers between devices with their start and end apart: 3, of which 2 were waited for; matrix products, arithmetic and copies ran while one was open for 16% of the time, Pallas kernels for 0%

profile of v1, /device:TPU:16, one launch (start us, length us, event | category | flops | bytes accessed | tf_op | source)
XLA Modules:
  0.0 296.2 jit_solution(5951758645161607549)
XLA Ops:
  0.6 2.7 stack.2
  3.4 10.0 %all-to-all-start = ((bf16[16,1,64,1024]{3,2,1,0:T(8,128)(2,1)}), bf16[16,1,64,1024]{3,2,1,0:T(8,128)(2,1)}, u32[]{:S(2)}, u32[]{:S(2)}) async-start(bf16[16,1,64,1024]{3,2,1,0:T(8,128)(2,1)} %stack.2), calls=%async_computation | async-start | bytes 4194304 | tf_op jit(solution)/shard_map/all_to_all | solution.py:23
  14.5 1.3 dynamic-slice
  16.7 53.6 %all-reduce = s32[1152]{0:T(1024)S(1)} all-reduce(s32[1152]{0:T(1024)S(1)} %add_dynamic-update-slice_fusion), channel_id=1, replica_groups=mesh['blk'=16,'exp'=32] {'blk'}, use_global_device_ids=true, to_apply=%add | all-reduce | flops 1152 | bytes 9216
  71.0 0.8 copy.57
  71.8 9.0 %reduce-window.19 = s32[32,8,128]{2,1,0:T(8,128)S(1)} reduce-window(s32[32,8,128]{2,1,0:T(8,128)S(1)} %fusion.45, s32[]{:T(128)} %constant.83.clone.1), window={size=1x1x128 pad=0_0x0_0x127_0}, to_apply=%region_6.7 | reduce-window | flops 4161536 | bytes 262148 | tf_op jit(solution)/shard_map/reduce-window.1
  81.3 1.6 broadcast_in_dim.111
  82.8 13.6 %all-to-all-start.1 = ((bf16[32,32,1024]{2,1,0:T(8,128)(2,1)}), bf16[32,32,1024]{2,1,0:T(8,128)(2,1)}, u32[]{:S(2)}, u32[]{:S(2)}) async-start(bf16[32,32,1024]{2,1,0:T(8,128)(2,1)} %broadcast_in_dim.111), calls=%async_computation.1 | async-start | bytes 4194304 | tf_op jit(solution)/shard_map/all_to_all | solution.py:42
  96.7 5.3 %fusion.5 = pred[1280,128]{1,0:T(8,128)(4,1)} fusion(s32[128,8]{0,1:T(8,128)S(1)} %copy.68), kind=kLoop, calls=%fused_computation.11 | loop fusion | flops 2457600 | bytes 167936 | tf_op jit(solution)/shard_map/reduce_or | solution.py:133
  102.2 1.3 select_reduce_fusion.1
  103.5 2.7 fusion.58
  106.2 1.3 copy.60
  107.6 1.5 copy.59
  109.1 2.2 fusion
  111.3 0.2 fusion.31
  111.5 2.2 fusion.3
  113.8 1.5 fusion.15
  115.4 0.3 fusion.23
  115.7 31.0 %all-to-all-done.1 = bf16[32,32,1024]{2,1,0:T(8,128)(2,1)} async-done(((bf16[32,32,1024]{2,1,0:T(8,128)(2,1)}), bf16[32,32,1024]{2,1,0:T(8,128)(2,1)}, u32[]{:S(2)}, u32[]{:S(2)}) %all-to-all-start.1) | async-done | bytes 2097184 | tf_op jit(solution)/shard_map/all_to_all | solution.py:42
  146.8 2.1 multiply_reduce_fusion
  148.9 0.9 convolution_convert_fusion.1
  149.8 69.1 %all_to_all.20 = bf16[32,40,1024]{2,1,0:T(8,128)(2,1)S(1)} all-to-all(bf16[32,40,1024]{2,1,0:T(8,128)(2,1)S(1)} %bitcast.121), channel_id=1, replica_groups=mesh['blk'=16,'exp'=32] {'exp'}, dimensions={0} | all-to-all | bytes 5242880 | tf_op jit(solution)/shard_map/all_to_all | solution.py:136
  219.0 2.9 fusion.10
  221.9 3.1 %convolution_convert_fusion = bf16[1280,1024]{1,0:T(8,128)(2,1)} fusion(f32[1280,1024]{1,0:T(8,128)S(1)} %fusion.10, bf16[1,512,1024]{2,1,0:T(8,128)(2,1)S(1)} %copy-done.13), kind=kOutput, calls=%fused_computation.14 | convolution fusion | flops 1347420160 | bytes 8912896 | tf_op jit(solution)/shard_map/dot_general | solution.py:142
  225.0 4.9 %all-to-all-start.3 = ((bf16[32,40,1024]{2,1,0:T(8,128)(2,1)}), bf16[32,40,1024]{2,1,0:T(8,128)(2,1)}, u32[]{:S(2)}, u32[]{:S(2)}) async-start(bf16[32,40,1024]{2,1,0:T(8,128)(2,1)} %bitcast.123), calls=%async_computation.3 | async-start | bytes 5242880 | tf_op jit(solution)/shard_map/all_to_all | solution.py:147
  230.4 0.4 select_reduce_fusion.2
  231.0 6.6 %gather_fusion = s32[1024]{0:T(1024)S(1)} fusion(s32[128]{0:T(128)S(1)} %reshape.285, s32[1024]{0:T(1024)S(1)} %broadcast_clamp_fusion), kind=kCustom, calls=%fused_computation | custom fusion | bytes 12288 | tf_op jit(solution)/shard_map/gather | solution.py:171
  237.7 1.6 select_reduce_fusion
  239.3 1.8 copy.69
  241.1 3.1 %fusion.14 = bf16[1,256,1024]{2,1,0:T(8,128)(2,1)} fusion(bf16[1024,1024]{1,0:T(8,128)(2,1)} %bitcast.42, s32[1024]{0:T(1024)S(1)} %add_select_fusion.1, s32[1024]{0:T(1024)S(1)} %gather_fusion, s32[256]{0:T(256)S(1)} %get-tuple-element.30, s32[256]{0:T(256)S(1)} %get-tuple-element.31), kind=kOutput, calls=%fused_computation.24 | convolution fusion | flops 537919488 | bytes 2631680 | tf_op jit(solution)/shard_map/dot_general | solution.py:172
  244.2 48.7 %all-to-all-done.3 = bf16[32,40,1024]{2,1,0:T(8,128)(2,1)} async-done(((bf16[32,40,1024]{2,1,0:T(8,128)(2,1)}), bf16[32,40,1024]{2,1,0:T(8,128)(2,1)}, u32[]{:S(2)}, u32[]{:S(2)}) %all-to-all-start.3) | async-done | bytes 2621472 | tf_op jit(solution)/shard_map/all_to_all | solution.py:147
  292.9 3.3 %fusion.26 = bf16[1,128,1024]{2,1,0:T(8,128)(2,1)} fusion(f32[128,1024]{1,0:T(8,128)S(1)} %get-tuple-element.29, f32[128,1280]{1,0:T(8,128)S(1)} %select_reduce_fusion, bf16[1280,1024]{1,0:T(8,128)(2,1)} %bitcast.39), kind=kOutput, calls=%fused_computation.36 | convolution fusion | flops 1006895104 | bytes 4063232 | tf_op jit(solution)/shard_map/dot_general | solution.py:154
  (78 shorter events, 2.8 us)
Async XLA Ops:
  0.6 218.3 %copy-start = (bf16[1,1024,1024]{2,1,0:T(8,128)(2,1)S(1)}, bf16[1,1024,1024]{2,1,0:T(8,128)(2,1)}, u32[]{:S(2)}) copy-start(bf16[1,1024,1024]{2,1,0:T(8,128)(2,1)} %param.23) | copy-start | bytes 6291460
  3.3 10.1 %copy-start.10 = (s32[1,128,8]{1,2,0:T(8,128)S(1)}, s32[1,128,8]{1,2,0:T(8,128)}, u32[]{:S(2)}) copy-start(s32[1,128,8]{1,2,0:T(8,128)} %param.21) | copy-start | bytes 12292
  3.3 10.4 %copy-start.14 = (s32[1,2]{1,0:T(1,128)S(1)}, s32[1,2]{1,0:T(1,128)}, u32[]{:S(2)}) copy-start(s32[1,2]{1,0:T(1,128)} %param.18) | copy-start | bytes 28
  3.3 13.1 %copy-start.12 = (s32[1,8,1]{1,2,0:T(1,128)S(1)}, s32[1,8,1]{1,2,0:T(1,128)}, u32[]{:S(2)}) copy-start(s32[1,8,1]{1,2,0:T(1,128)} %param.25) | copy-start | bytes 100
  3.3 67.2 %copy-start.5 = (bf16[1,128,1024]{2,1,0:T(8,128)(2,1)S(1)}, bf16[1,128,1024]{2,1,0:T(8,128)(2,1)}, u32[]{:S(2)}) copy-start(bf16[1,128,1024]{2,1,0:T(8,128)(2,1)} %param.14) | copy-start | bytes 786436
  3.3 67.3 %copy-start.15 = (s32[1,1,4]{2,1,0:T(1,128)S(1)}, s32[1,1,4]{2,1,0:T(1,128)}, u32[]{:S(2)}) copy-start(s32[1,1,4]{2,1,0:T(1,128)} %param.19) | copy-start | bytes 52
  3.3 67.5 %copy-start.6 = (bf16[1,128,1024]{2,1,0:T(8,128)(2,1)S(1)}, bf16[1,128,1024]{2,1,0:T(8,128)(2,1)}, u32[]{:S(2)}) copy-start(bf16[1,128,1024]{2,1,0:T(8,128)(2,1)} %param.15) | copy-start | bytes 786436
  3.3 77.9 %copy-start.9 = (bf16[32,1024]{1,0:T(8,128)(2,1)S(1)}, bf16[32,1024]{1,0:T(8,128)(2,1)}, u32[]{:S(2)}) copy-start(bf16[32,1024]{1,0:T(8,128)(2,1)} %param.20) | copy-start | bytes 196612
  3.4 77.9 %all-to-all-start = ((bf16[16,1,64,1024]{3,2,1,0:T(8,128)(2,1)}), bf16[16,1,64,1024]{3,2,1,0:T(8,128)(2,1)}, u32[]{:S(2)}, u32[]{:S(2)}) async-start(bf16[16,1,64,1024]{3,2,1,0:T(8,128)(2,1)} %stack.2), calls=%async_computation | async-start | bytes 4194304 | tf_op jit(solution)/shard_map/all_to_all | solution.py:23
  82.8 63.9 %all-to-all-start.1 = ((bf16[32,32,1024]{2,1,0:T(8,128)(2,1)}), bf16[32,32,1024]{2,1,0:T(8,128)(2,1)}, u32[]{:S(2)}, u32[]{:S(2)}) async-start(bf16[32,32,1024]{2,1,0:T(8,128)(2,1)} %broadcast_in_dim.111), calls=%async_computation.1 | async-start | bytes 4194304 | tf_op jit(solution)/shard_map/all_to_all | solution.py:42
  109.0 2.2 copy-start.1
  111.5 2.3 copy-start.2
  113.8 1.6 copy-start.8
  115.3 31.4 %copy-start.7 = (bf16[1,128,1024]{2,1,0:T(8,128)(2,1)S(1)}, bf16[1,128,1024]{2,1,0:T(8,128)(2,1)}, u32[]{:S(2)}) copy-start(bf16[1,128,1024]{2,1,0:T(8,128)(2,1)} %param.13) | copy-start | bytes 786436
  115.4 33.5 %copy-start.4 = (pred[1280,128]{1,0:T(8,128)(4,1)S(1)}, pred[1280,128]{1,0:T(8,128)(4,1)}, u32[]{:S(2)}) copy-start(pred[1280,128]{1,0:T(8,128)(4,1)} %fusion.5) | copy-start | bytes 491524
  115.7 34.1 %copy-start.3 = (bf16[128,8,2,64]{0,3,2,1:T(8,128)(2,1)}, bf16[128,8,2,64]{0,3,2,1:T(8,128)(2,1)S(1)}, u32[]{:S(2)}) copy-start(bf16[128,8,2,64]{0,3,2,1:T(8,128)(2,1)S(1)} %fusion.23) | copy-start | bytes 786436
  219.0 2.9 copy-start.13
  225.0 5.1 %copy-start.11 = (f32[1,128,8]{1,2,0:T(8,128)S(1)}, f32[1,128,8]{1,2,0:T(8,128)}, u32[]{:S(2)}) copy-start(f32[1,128,8]{1,2,0:T(8,128)} %param.22) | copy-start | bytes 12292
  225.0 67.9 %all-to-all-start.3 = ((bf16[32,40,1024]{2,1,0:T(8,128)(2,1)}), bf16[32,40,1024]{2,1,0:T(8,128)(2,1)}, u32[]{:S(2)}, u32[]{:S(2)}) async-start(bf16[32,40,1024]{2,1,0:T(8,128)(2,1)} %bitcast.123), calls=%async_computation.3 | async-start | bytes 5242880 | tf_op jit(solution)/shard_map/all_to_all | solution.py:147
